TPU v7x, 512 devices: a whole 4x8x8 slice. The times are simulated.
512 devices in a mesh: dp: 8 (over z), cent: 64 (over x, y, core).
Axes of the slice: x: 4, y: 8, z: 8, core: 2. Of those that a mesh axis runs over, the one named last changes fastest.
Arguments:
- points: bfloat16 [24576, 1024], P(('dp', 'cent')), may hold values from -6 to 6
- assign: int32 [24576], P(('dp', 'cent')), may hold values from 0 to 32767, as said below
- centroids: float32 [32768, 1024], P('cent'), may hold values from -6 to 6
- counts: int32 [32768], P('cent'), may hold values from 1 to 4
Outputs:
- new_centroids: float32 [32768, 1024], P('cent')
- best: float32 [24576], P(('dp', 'cent'))
Inputs may be any that keep to these rules, and one draw needn't show every extreme that they name: `assign`: split the points into aligned blocks of 3072 points in order (the points of one dp index). In every block, the clusters k * 512 to (k + 1) * 512 - 1 receive exactly 48 points together, for every k.
All inputs are finite; a program needn't handle non-finite values.
Results may differ from a plain program's by a relative error of at most 0.0003.
Values may be sent and summed in bfloat16 or wider, within the bound.
No kernel may reach another device: no remote copies, remote signals or barrier semaphores. Data moves between devices by JAX's collectives and lax.ppermute only.
A program may use at most 128 MiB of HBM per device.

v0:
```python
import jax
import jax.numpy as jnp
from jax import lax
from jax.sharding import PartitionSpec as P


def renorm(merged):
    return merged * lax.rsqrt(jnp.mean(merged * merged, axis=1, keepdims=True) + 1e-05)


def make_per_device(ncent):

    def per_device(points, assign, centroids, counts):
        kdev = centroids.shape[0]
        pdev, width = points.shape
        first = lax.axis_index("cent") * kdev
        weighted = centroids * counts.astype(jnp.float32)[:, None]
        rows = lax.all_gather(points, "cent", axis=0, tiled=True)
        labels = lax.all_to_all(
            jnp.broadcast_to(assign[None], (ncent, pdev)), "cent", 0, 0, tiled=True
        ).reshape(-1)
        local = labels - first
        mine = (local >= 0) & (local < kdev)
        rank = jnp.cumsum(mine.astype(jnp.int32)) - 1
        pick = mine[None, :] & (rank[None, :] == jnp.arange(pdev, dtype=jnp.int32)[:, None])
        where = jnp.sum(
            jnp.where(pick, jnp.arange(rows.shape[0], dtype=jnp.int32)[None, :], 0), axis=1
        )
        picked = jnp.take(rows, where, axis=0)
        picked_label = jnp.take(local, where, axis=0)
        hi = (picked_label // 16).astype(jnp.bfloat16)
        lo = (picked_label % 16).astype(jnp.bfloat16)
        packed = jnp.concatenate(
            [
                picked.astype(jnp.bfloat16),
                hi[:, None],
                lo[:, None],
                jnp.zeros((pdev, 126), jnp.bfloat16),
            ],
            axis=1,
        )
        gathered = lax.all_gather(packed, "dp", axis=0, tiled=True)
        grows = gathered[:, :width]
        glabel = gathered[:, width].astype(jnp.int32) * 16 + gathered[:, width + 1].astype(
            jnp.int32
        )
        onehot = (glabel[None, :] == jnp.arange(kdev, dtype=jnp.int32)[:, None]).astype(
            jnp.bfloat16
        )
        total = jnp.dot(onehot, grows, preferred_element_type=jnp.float32)
        fresh = renorm(weighted + total)
        rounded = fresh.astype(jnp.bfloat16)
        scores = jnp.dot(rows, rounded.T, preferred_element_type=jnp.float32)
        local_best = jnp.max(scores.reshape(ncent, pdev, kdev), axis=2)
        received = lax.all_to_all(local_best, "cent", 0, 0, tiled=True)
        values = points.astype(jnp.float32)
        scale = width * jnp.sqrt(jnp.mean(values * values, axis=1) + 1e-06)
        return (fresh, jnp.max(received / scale[None, :], axis=0))

    return per_device


def solution(mesh):
    placed = (P(("dp", "cent"), None), P(("dp", "cent")), P("cent", None), P("cent"))
    return jax.shard_map(
        make_per_device(mesh.shape["cent"]),
        mesh=mesh,
        in_specs=placed,
        out_specs=(P("cent", None), P(("dp", "cent"))),
        check_vma=False,
    )
```

profile of v0, /device:TPU:1, one launch (start us, length us, event | category | flops | bytes accessed | tf_op | source)
XLA Modules:
  0.0 165.8 jit_solution(1306409276618937855)
XLA Ops:
  7.2 0.7 all-gather.2.cloned.1.call-update
  7.9 1.3 broadcast_in_dim.32
  9.2 11.6 %all-to-all-start = ((s32[64,1,48]{2,1,0:T(1,128)}), s32[64,1,48]{2,1,0:T(1,128)S(1)}, u32[]{:S(2)}, u32[]{:S(2)}) async-start(s32[64,1,48]{2,1,0:T(1,128)} %broadcast_in_dim.32), calls=%async_computation | async-start | bytes 65536 | tf_op jit(solution)/shard_map/all_to_all | solution.py:19
  20.8 1.0 multiply_reduce_fusion.1
  21.8 0.7 convert_element_type.53
  22.5 7.5 %all-to-all-done = s32[64,1,48]{2,1,0:T(1,128)S(1)} async-done(((s32[64,1,48]{2,1,0:T(1,128)}), s32[64,1,48]{2,1,0:T(1,128)S(1)}, u32[]{:S(2)}, u32[]{:S(2)}) %all-to-all-start) | async-done | bytes 12320 | tf_op jit(solution)/shard_map/all_to_all | solution.py:19
  30.1 0.2 subtract_reduce_fusion
  30.3 0.1 reshape.215
  30.3 0.3 reduce-window.9
  30.6 0.1 slice.25
  30.7 0.1 sub.29
  30.8 0.1 slice_reduce_fusion
  30.9 0.1 add_bitcast_fusion
  31.0 0.2 select_reduce_fusion
  31.3 0.1 copy.19
  31.4 0.1 fusion.8
  31.5 0.8 gather_fusion.1
  32.3 0.1 copy.22
  32.4 70.5 %all-gather.2.cloned.1.call-done = bf16[3072,1024]{1,0:T(8,128)(2,1)} async-done(((bf16[48,1024]{1,0:T(8,128)(2,1)}), bf16[3072,1024]{1,0:T(8,128)(2,1)}) %all-gather.2.cloned.1.call-update) | async-done | bytes 6291472 | tf_op jit(solution)/shard_map/all_gather | solution.py:18
  103.0 4.3 %gather_fusion = bf16[48,1024]{1,0:T(8,128)(2,1)S(1)} fusion(bf16[3072,1024]{1,0:T(8,128)(2,1)} %all-gather.2.cloned.1.call-done, s32[1024]{0:T(1024)S(1)} %pad_clamp_fusion), kind=kCustom, calls=%fused_computation | custom fusion | bytes 196800 | tf_op jit(solution)/shard_map/jit(_take)/gather | solution.py:29
  107.3 0.1 broadcast_select_fusion
  107.4 0.1 concatenate.3
  107.5 23.1 %all_gather.7 = bf16[384,1152]{1,0:T(8,128)(2,1)S(1)} all-gather(bf16[48,1152]{1,0:T(8,128)(2,1)S(1)} %concatenate.3), channel_id=1, replica_groups=mesh['dp'=8,'cent'=64] {'dp'}, dimensions={0}, use_global_device_ids=true | all-gather | bytes 995328 | tf_op jit(solution)/shard_map/all_gather | solution.py:42
  130.5 0.2 add_reduce_fusion
  130.8 0.8 multiply_reduce_fusion
  131.6 0.2 broadcast_multiply_fusion
  131.8 1.7 %copy-done.2 = bf16[3072,1024]{1,0:T(8,128)(2,1)S(1)} copy-done((bf16[3072,1024]{1,0:T(8,128)(2,1)S(1)}, bf16[3072,1024]{1,0:T(8,128)(2,1)}, u32[]{:S(2)}) %copy-start.2) | copy-done | bytes 6291480
  133.6 3.8 %convolution_reduce_fusion = f32[3072]{0:T(1024)S(1)} fusion(bf16[3072,1024]{1,0:T(8,128)(2,1)S(1)} %copy-done.2, f32[512,1024]{1,0:T(8,128)S(1)} %broadcast_multiply_fusion), kind=kOutput, calls=%fused_computation.4 | convolution fusion | flops 3223319552 | bytes 8400896 | tf_op jit(solution)/shard_map/dot_general | solution.py:53
  137.3 0.7 all_to_all.13
  138.0 11.1 %all-to-all-start.1 = ((f32[64,1,48]{2,1,0:T(1,128)}), f32[64,1,48]{2,1,0:T(1,128)S(1)}, u32[]{:S(2)}, u32[]{:S(2)}) async-start(f32[64,1,48]{2,1,0:T(1,128)} %bitcast.3), calls=%async_computation.1 | async-start | bytes 65536 | tf_op jit(solution)/shard_map/all_to_all | solution.py:55
  149.1 9.3 %all-to-all-done.1 = f32[64,1,48]{2,1,0:T(1,128)S(1)} async-done(((f32[64,1,48]{2,1,0:T(1,128)}), f32[64,1,48]{2,1,0:T(1,128)S(1)}, u32[]{:S(2)}, u32[]{:S(2)}) %all-to-all-start.1) | async-done | bytes 12320 | tf_op jit(solution)/shard_map/all_to_all | solution.py:55
  158.4 0.5 divide_reduce_fusion
  (14 shorter events, 0.2 us)
Async XLA Ops:
  7.2 123.6 %copy-start.1 = (f32[512,1024]{1,0:T(8,128)S(1)}, f32[512,1024]{1,0:T(8,128)}, u32[]{:S(2)}) copy-start(f32[512,1024]{1,0:T(8,128)} %param.6) | copy-start | bytes 6291460
  7.2 95.8 %all-gather.2.cloned.1.call-start = ((), (), s32[]{:S(2)}) async-start(), calls=%async_computation.2 | async-start | bytes 6389760 | tf_op jit(solution)/shard_map/all_gather | solution.py:18
  9.2 20.9 %all-to-all-start = ((s32[64,1,48]{2,1,0:T(1,128)}), s32[64,1,48]{2,1,0:T(1,128)S(1)}, u32[]{:S(2)}, u32[]{:S(2)}) async-start(s32[64,1,48]{2,1,0:T(1,128)} %broadcast_in_dim.32), calls=%async_computation | async-start | bytes 65536 | tf_op jit(solution)/shard_map/all_to_all | solution.py:19
  130.8 2.8 %copy-start.2 = (bf16[3072,1024]{1,0:T(8,128)(2,1)S(1)}, bf16[3072,1024]{1,0:T(8,128)(2,1)}, u32[]{:S(2)}) copy-start(bf16[3072,1024]{1,0:T(8,128)(2,1)} %all-gather.2.cloned.1.call-done) | copy-start | bytes 18874372
  133.6 3.8 %copy-start = (f32[512,1024]{1,0:T(8,128)}, f32[512,1024]{1,0:T(8,128)S(1)}, u32[]{:S(2)}) copy-start(f32[512,1024]{1,0:T(8,128)S(1)} %broadcast_multiply_fusion) | copy-start | bytes 6291460
  138.0 20.4 %all-to-all-start.1 = ((f32[64,1,48]{2,1,0:T(1,128)}), f32[64,1,48]{2,1,0:T(1,128)S(1)}, u32[]{:S(2)}, u32[]{:S(2)}) async-start(f32[64,1,48]{2,1,0:T(1,128)} %bitcast.3), calls=%async_computation.1 | async-start | bytes 65536 | tf_op jit(solution)/shard_map/all_to_all | solution.py:55
Sparse Core Ops, SparseCore 0:
  11.3 91.5 all-gather.1
where the time goes:
time: 166 us
  waiting for transfers between devices  88.1 us (53%)
  blocking collectives  23.1 us (14%)
  starting transfers between devices  22.7 us (14%)
  between operations  14.2 us (9%)
  local copies, waits for them, and re-layouts  9.42 us (6%)
  matrix products  4.59 us (3%)
  other arithmetic  3.79 us (2%)
    all_gather x1, waiting for transfers between devices, per_device(): rows = lax.all_gather(points, 'cent', axis=0, tiled=True)  70.5 us
    all_gather x1, blocking collectives, per_device(): gathered = lax.all_gather(packed, 'dp', axis=0, tiled=True)  23.1 us
    all_to_all x1, starting transfers between devices, per_device(): lax.all_to_all(jnp.broadcast_to(assign[None], (ncent, pdev)), 'cent', 0,...  11.6 us
    all_to_all x1, starting transfers between devices, per_device(): received = lax.all_to_all(local_best, 'cent', 0, 0, tiled=True)  11.1 us
    all_to_all x1, waiting for transfers between devices, per_device(): received = lax.all_to_all(local_best, 'cent', 0, 0, tiled=True)  9.3 us
    all_to_all x1, waiting for transfers between devices, per_device(): lax.all_to_all(jnp.broadcast_to(assign[None], (ncent, pdev)), 'cent', 0,...  7.53 us
    gather x1, local copies, waits for them, and re-layouts, per_device(): picked = jnp.take(rows, where, axis=0)  4.32 us
    dot_general x1, matrix products, per_device(): scores = jnp.dot(rows, rounded.T, preferred_element_type=jnp.float32)  3.76 us
  transfers between devices with their start and end apart: 3, of which 3 were waited for; matrix products, arithmetic and copies ran while one was open for 3% of the time, Pallas kernels for 0%

commit v1 on v0

--- a/solution.py
+++ b/solution.py
@@ -39,7 +39,9 @@
             ],
             axis=1,
         )
-        gathered = lax.all_gather(packed, "dp", axis=0, tiled=True)
+        gathered = jnp.concatenate(
+            lax.all_to_all(jnp.stack([packed] * lax.axis_size("dp")), "dp", 0, 0), axis=0
+        )
         grows = gathered[:, :width]
         glabel = gathered[:, width].astype(jnp.int32) * 16 + gathered[:, width + 1].astype(
             jnp.int32

time: 166 us -> 174 us (1.048)
  waiting for transfers between devices: 88.1 us -> 115 us
  blocking collectives: 23.1 us -> 0 us
  matrix products: 4.59 us -> 8.07 us
  starting transfers between devices: 22.7 us -> 24.8 us
    all_to_all x0 -> x1, waiting for transfers between devices: none -> 25.5 us  [per_device(): lax.all_to_all(jnp.stack([packed] * lax.axis_size('dp')), 'dp', 0, 0)]
    all_gather x1 -> x0, blocking collectives: 23.1 us -> none  [per_device(): gathered = lax.all_gather(packed, 'dp', axis=0, tiled=True)]
    all_to_all x0 -> x1, starting transfers between devices: none -> 7.1 us  [per_device(): lax.all_to_all(jnp.stack([packed] * lax.axis_size('dp')), 'dp', 0, 0)]
    all_to_all x1, starting transfers between devices: 11.1 us -> 6.05 us  [per_device(): received = lax.all_to_all(local_best, 'cent', 0, 0, tiled=True)]
    dot_general x1, matrix products: 3.76 us -> 7.24 us  [per_device(): scores = jnp.dot(rows, rounded.T, preferred_element_type=jnp.float32)]
  transfers between devices with their start and end apart: 3 -> 4, of which waited for: 3 -> 4; matrix products, arithmetic and copies ran while one was open for 3% -> 2% of each run, Pallas kernels for 0% -> 0%
where the time goes in v1:
time: 174 us; the launch traced here: 173 us
  waiting for transfers between devices  115 us (66%)
  starting transfers between devices  24.8 us (14%)
  between operations  14.2 us (8%)
  local copies, waits for them, and re-layouts  8.69 us (5%)
  matrix products  8.07 us (5%)
  other arithmetic  2.21 us (1%)
    all_gather x1, waiting for transfers between devices, per_device(): rows = lax.all_gather(points, 'cent', axis=0, tiled=True)  70.5 us
    all_to_all x1, waiting for transfers between devices, per_device(): lax.all_to_all(jnp.stack([packed] * lax.axis_size('dp')), 'dp', 0, 0)  25.5 us
    all_to_all x1, starting transfers between devices, per_device(): lax.all_to_all(jnp.broadcast_to(assign[None], (ncent, pdev)), 'cent', 0,...  11.6 us
    all_to_all x1, waiting for transfers between devices, per_device(): received = lax.all_to_all(local_best, 'cent', 0, 0, tiled=True)  9.3 us
    all_to_all x1, waiting for transfers between devices, per_device(): lax.all_to_all(jnp.broadcast_to(assign[None], (ncent, pdev)), 'cent', 0,...  9.24 us
    dot_general x1, matrix products, per_device(): scores = jnp.dot(rows, rounded.T, preferred_element_type=jnp.float32)  7.24 us
    all_to_all x1, starting transfers between devices, per_device(): lax.all_to_all(jnp.stack([packed] * lax.axis_size('dp')), 'dp', 0, 0)  7.1 us
    all_to_all x1, starting transfers between devices, per_device(): received = lax.all_to_all(local_best, 'cent', 0, 0, tiled=True)  6.05 us
  transfers between devices with their start and end apart: 4, of which 4 were waited for; matrix products, arithmetic and copies ran while one was open for 2% of the time, Pallas kernels for 0%

profile of v1, /device:TPU:1, one launch (start us, length us, event | category | flops | bytes accessed | tf_op | source)
XLA Modules:
  0.0 173.2 jit_solution(11182857427663340190)
XLA Ops:
  7.2 0.7 all-gather.2.cloned.1.call-update
  7.9 1.3 broadcast_in_dim.32
  9.2 11.6 %all-to-all-start = ((s32[64,1,48]{2,1,0:T(1,128)}), s32[64,1,48]{2,1,0:T(1,128)S(1)}, u32[]{:S(2)}, u32[]{:S(2)}) async-start(s32[64,1,48]{2,1,0:T(1,128)} %broadcast_in_dim.32), calls=%async_computation | async-start | bytes 65536 | tf_op jit(solution)/shard_map/all_to_all | solution.py:19
  20.8 9.2 %all-to-all-done = s32[64,1,48]{2,1,0:T(1,128)S(1)} async-done(((s32[64,1,48]{2,1,0:T(1,128)}), s32[64,1,48]{2,1,0:T(1,128)S(1)}, u32[]{:S(2)}, u32[]{:S(2)}) %all-to-all-start) | async-done | bytes 12320 | tf_op jit(solution)/shard_map/all_to_all | solution.py:19
  30.0 0.2 subtract_reduce_fusion
  30.3 0.1 reshape.221
  30.3 0.3 reduce-window.9
  30.6 0.1 slice.25
  30.7 0.1 sub.29
  30.8 0.1 slice_reduce_fusion
  30.9 0.1 add_bitcast_fusion
  31.0 0.2 select_reduce_fusion
  31.3 0.1 copy.24
  31.4 0.1 fusion.8
  31.5 0.8 gather_fusion.1
  32.3 0.1 copy.27
  32.4 70.5 %all-gather.2.cloned.1.call-done = bf16[3072,1024]{1,0:T(8,128)(2,1)} async-done(((bf16[48,1024]{1,0:T(8,128)(2,1)}), bf16[3072,1024]{1,0:T(8,128)(2,1)}) %all-gather.2.cloned.1.call-update) | async-done | bytes 6291472 | tf_op jit(solution)/shard_map/all_gather | solution.py:18
  102.9 4.3 %gather_fusion = bf16[48,1024]{1,0:T(8,128)(2,1)S(1)} fusion(bf16[3072,1024]{1,0:T(8,128)(2,1)} %all-gather.2.cloned.1.call-done, s32[1024]{0:T(1024)S(1)} %pad_clamp_fusion), kind=kCustom, calls=%fused_computation | custom fusion | bytes 196800 | tf_op jit(solution)/shard_map/jit(_take)/gather | solution.py:29
  107.3 0.1 broadcast_select_fusion
  107.4 0.1 concatenate.3
  107.5 1.0 stack.2
  108.4 7.1 %all-to-all-start.1 = ((bf16[8,48,1152]{2,1,0:T(8,128)(2,1)}), bf16[8,48,1152]{2,1,0:T(8,128)(2,1)S(1)}, u32[]{:S(2)}, u32[]{:S(2)}) async-start(bf16[8,48,1152]{2,1,0:T(8,128)(2,1)} %stack.2), calls=%async_computation.1 | async-start | bytes 1769472 | tf_op jit(solution)/shard_map/all_to_all | solution.py:43
  115.6 0.1 multiply_reduce_fusion.1
  115.7 25.5 %all-to-all-done.1 = bf16[8,48,1152]{2,1,0:T(8,128)(2,1)S(1)} async-done(((bf16[8,48,1152]{2,1,0:T(8,128)(2,1)}), bf16[8,48,1152]{2,1,0:T(8,128)(2,1)S(1)}, u32[]{:S(2)}, u32[]{:S(2)}) %all-to-all-start.1) | async-done | bytes 884768 | tf_op jit(solution)/shard_map/all_to_all | solution.py:43
  141.2 0.2 add_reduce_fusion
  141.5 0.8 multiply_reduce_fusion
  142.3 0.2 broadcast_multiply_fusion
  142.5 7.2 %convolution_reduce_fusion = f32[3072]{0:T(1024)S(1)} fusion(bf16[3072,1024]{1,0:T(8,128)(2,1)} %all-gather.2.cloned.1.call-done, f32[512,1024]{1,0:T(8,128)S(1)} %broadcast_multiply_fusion), kind=kOutput, calls=%fused_computation.4 | convolution fusion | flops 3223319552 | bytes 8400896 | tf_op jit(solution)/shard_map/dot_general | solution.py:55
  149.8 0.7 all_to_all.17
  150.5 6.0 %all-to-all-start.2 = ((f32[64,1,48]{2,1,0:T(1,128)}), f32[64,1,48]{2,1,0:T(1,128)S(1)}, u32[]{:S(2)}, u32[]{:S(2)}) async-start(f32[64,1,48]{2,1,0:T(1,128)} %bitcast.4), calls=%async_computation.2 | async-start | bytes 65536 | tf_op jit(solution)/shard_map/all_to_all | solution.py:57
  156.5 9.3 %all-to-all-done.2 = f32[64,1,48]{2,1,0:T(1,128)S(1)} async-done(((f32[64,1,48]{2,1,0:T(1,128)}), f32[64,1,48]{2,1,0:T(1,128)S(1)}, u32[]{:S(2)}, u32[]{:S(2)}) %all-to-all-start.2) | async-done | bytes 12320 | tf_op jit(solution)/shard_map/all_to_all | solution.py:57
  165.8 0.5 divide_reduce_fusion
  (18 shorter events, 0.2 us)
Async XLA Ops:
  7.2 95.8 %all-gather.2.cloned.1.call-start = ((), (), s32[]{:S(2)}) async-start(), calls=%async_computation.3 | async-start | bytes 6389760 | tf_op jit(solution)/shard_map/all_gather | solution.py:18
  9.2 20.9 %all-to-all-start = ((s32[64,1,48]{2,1,0:T(1,128)}), s32[64,1,48]{2,1,0:T(1,128)S(1)}, u32[]{:S(2)}, u32[]{:S(2)}) async-start(s32[64,1,48]{2,1,0:T(1,128)} %broadcast_in_dim.32), calls=%async_computation | async-start | bytes 65536 | tf_op jit(solution)/shard_map/all_to_all | solution.py:19
  32.4 83.2 %copy-start.3 = (s32[512]{0:T(512)S(1)}, s32[512]{0:T(512)}, u32[]{:S(2)}) copy-start(s32[512]{0:T(512)} %param.7) | copy-start | bytes 6148
  32.4 83.2 %copy-start.2 = (bf16[48,1024]{1,0:T(8,128)(2,1)S(1)}, bf16[48,1024]{1,0:T(8,128)(2,1)}, u32[]{:S(2)}) copy-start(bf16[48,1024]{1,0:T(8,128)(2,1)} %param.4) | copy-start | bytes 294916
  32.4 109.0 %copy-start.1 = (f32[512,1024]{1,0:T(8,128)S(1)}, f32[512,1024]{1,0:T(8,128)}, u32[]{:S(2)}) copy-start(f32[512,1024]{1,0:T(8,128)} %param.6) | copy-start | bytes 6291460
  108.4 32.8 %all-to-all-start.1 = ((bf16[8,48,1152]{2,1,0:T(8,128)(2,1)}), bf16[8,48,1152]{2,1,0:T(8,128)(2,1)S(1)}, u32[]{:S(2)}, u32[]{:S(2)}) async-start(bf16[8,48,1152]{2,1,0:T(8,128)(2,1)} %stack.2), calls=%async_computation.1 | async-start | bytes 1769472 | tf_op jit(solution)/shard_map/all_to_all | solution.py:43
  142.5 7.3 %copy-start = (f32[512,1024]{1,0:T(8,128)}, f32[512,1024]{1,0:T(8,128)S(1)}, u32[]{:S(2)}) copy-start(f32[512,1024]{1,0:T(8,128)S(1)} %broadcast_multiply_fusion) | copy-start | bytes 6291460
  150.5 15.4 %all-to-all-start.2 = ((f32[64,1,48]{2,1,0:T(1,128)}), f32[64,1,48]{2,1,0:T(1,128)S(1)}, u32[]{:S(2)}, u32[]{:S(2)}) async-start(f32[64,1,48]{2,1,0:T(1,128)} %bitcast.4), calls=%async_computation.2 | async-start | bytes 65536 | tf_op jit(solution)/shard_map/all_to_all | solution.py:57
Sparse Core Ops, SparseCore 0:
  11.3 91.5 all-gather.1
